TPU v7x, 32 devices: a whole 2x2x4 slice. The times are simulated.
32 devices in a mesh: expert: 16 (over z, y, core), dp: 2 (over x).
Axes of the slice: x: 2, y: 2, z: 4, core: 2. Of those that a mesh axis runs over, the one named last changes fastest.
Arguments:
- tokens: bfloat16 [4096, 2048], P(('expert', 'dp')), may hold values from -6 to 6
- cotangent: bfloat16 [4096, 2048], P(('expert', 'dp')), may hold values from -6 to 6
- expert_ids: int32 [4096, 6], P(('expert', 'dp')), may hold values from 0 to 15, all different within a row; in each aligned block of 128 rows (0 to 127, 128 to 255, ...) at most 60 rows name the same one
- gate_vals: float32 [4096, 6], P(('expert', 'dp')), may hold values from 0.05 to 0.5
- capacity: int32 [16], replicated, may hold values from 384 to 960
- w_gate: bfloat16 [16, 384, 2048], P('expert', 'dp'), may hold values from -0.125 to 0.125
- w_up: bfloat16 [16, 384, 2048], P('expert', 'dp'), may hold values from -0.125 to 0.125
- w_down: bfloat16 [16, 384, 2048], P('expert', 'dp'), may hold values from -0.3125 to 0.3125
Outputs:
- layer_out: bfloat16 [4096, 2048], P(('expert', 'dp'))
- grad_tokens: bfloat16 [4096, 2048], P(('expert', 'dp'))
- grad_gates: float32 [4096, 6], P(('expert', 'dp'))
- grad_gate_w: bfloat16 [16, 384, 2048], P('expert', 'dp')
- grad_up_w: bfloat16 [16, 384, 2048], P('expert', 'dp')
- grad_down_w: bfloat16 [16, 384, 2048], P('expert', 'dp')
Inputs may be any that keep to these rules, and one draw needn't show every extreme that they name: `expert_ids`: within the 128 rows of one device no expert is named more than 60 times, a bound that some block reaches.
All inputs are finite; a program needn't handle non-finite values.
Results may differ from a plain program's by a relative error of at most 0.0065.
Values may be sent and summed in bfloat16 or wider, within the bound.
No kernel may reach another device: no remote copies, remote signals or barrier semaphores. Data moves between devices by JAX's collectives and lax.ppermute only.
A program may use at most 128 MiB of HBM per device.

v0:
```python
import jax
import jax.numpy as jnp
import numpy as np
from jax import lax
from jax.sharding import Mesh
from jax.sharding import PartitionSpec as P


def shifted(value, axis, count, shift):
    return lax.ppermute(value, axis, [(j, (j + shift) % count) for j in range(count)])


def in_three(value):
    first = value.astype(jnp.bfloat16)
    rest = value - first.astype(jnp.float32)
    second = rest.astype(jnp.bfloat16)
    third = (rest - second.astype(jnp.float32)).astype(jnp.bfloat16)
    return jnp.concatenate([first, second, third], axis=0)


def on_device(tokens, cotangent, expert_ids, gate_vals, capacity, w_gate, w_up, w_down):
    tok_rows, width = tokens.shape
    top_count = expert_ids.shape[1]
    experts = capacity.shape[0]
    local_experts, hidden_part, _ = w_gate.shape
    slots = max(2, (5 * tok_rows * top_count + 4 * experts - 1) // (4 * experts))
    n_in = lax.axis_size("inner")
    n_dp = lax.axis_size("dp")
    half = lax.axis_index("half")
    inner = lax.axis_index("inner")
    source = half * n_in + inner
    n_src = 2 * n_in
    half_experts = n_in * local_experts
    half_rows = half_experts * slots
    weights = jnp.concatenate([w_gate, w_up, w_down], axis=0)
    pieces = [weights] + [shifted(weights, "dp", n_dp, d) for d in range(1, n_dp)]
    both_rows = jnp.concatenate([tokens, cotangent], axis=1)
    partner_rows = shifted(both_rows, "half", 2, 1)
    partner_gates = shifted(gate_vals, "half", 2, 1)
    flat_ids = expert_ids.reshape(-1)
    one_hot = (flat_ids[:, None] == jnp.arange(experts, dtype=jnp.int32)[None, :]).astype(jnp.int32)
    running = jnp.cumsum(one_hot, axis=0)
    local_rank = jnp.sum(running * one_hot, axis=1) - 1
    counts = running[-1]
    count_rows = jnp.where(
        jnp.arange(n_src, dtype=jnp.int32)[:, None] == source, counts[None, :], 0
    )
    all_counts = lax.psum(count_rows.astype(jnp.float32), ("half", "inner")).astype(jnp.int32)
    code = (flat_ids * slots + local_rank).reshape(tok_rows, top_count)
    partner_code = shifted(code, "half", 2, 1)
    all_rows = jnp.concatenate([both_rows, partner_rows], axis=0)
    all_gates = jnp.concatenate([gate_vals, partner_gates], axis=0)
    all_code = jnp.concatenate([code, partner_code], axis=0)
    local = all_code // slots - half * half_experts
    inside = (local >= 0) & (local < half_experts)
    side = (jnp.arange(2 * tok_rows, dtype=jnp.int32) >= tok_rows).astype(jnp.int32)[:, None]
    dest = jnp.where(inside, (local * 2 + side) * slots + all_code % slots, 2 * half_rows)
    row_of = jnp.broadcast_to(jnp.arange(2 * tok_rows, dtype=jnp.int32)[:, None], dest.shape)
    filled_by = (
        jnp.full((2 * half_rows,), -1, jnp.int32)
        .at[dest.reshape(-1)]
        .set(row_of.reshape(-1), mode="drop")
    )
    slot_gate = (
        jnp.zeros((2 * half_rows,), jnp.float32)
        .at[dest.reshape(-1)]
        .set(all_gates.reshape(-1), mode="drop")
    )
    pick = (filled_by[:, None] == jnp.arange(2 * tok_rows, dtype=jnp.int32)[None, :]).astype(
        jnp.bfloat16
    )
    picked = jnp.dot(pick, all_rows, preferred_element_type=jnp.float32)
    send_x = picked[:, :width].astype(jnp.bfloat16)
    send_c = (slot_gate[:, None] * picked[:, width:]).astype(jnp.bfloat16)
    send = jnp.concatenate([send_x, send_c], axis=1).reshape(half_experts, 2 * slots, 2 * width)
    got = lax.all_to_all(send, "inner", split_axis=0, concat_axis=0, tiled=True)
    got = got.reshape(n_in, local_experts, 2, slots, 2 * width)
    earlier = jnp.cumsum(all_counts, axis=0) - all_counts
    holders = jnp.arange(n_in, dtype=jnp.int32)[:, None]
    halves = jnp.stack([half, 1 - half])[None, :]
    sources = halves * n_in + holders
    mine = (half * n_in + inner) * local_experts + jnp.arange(local_experts, dtype=jnp.int32)
    before = earlier[sources][:, :, mine].transpose(0, 2, 1)
    ranks = jnp.arange(slots, dtype=jnp.int32)
    keep = before[..., None] + ranks < capacity[mine][None, :, None, None]
    got = jnp.where(keep[..., None], got, jnp.zeros((), got.dtype))
    got = got.transpose(1, 0, 2, 3, 4).reshape(local_experts, n_in * 2 * slots, 2 * width)
    rows_in = got[:, :, :width]
    rows_cot = got[:, :, width:]
    full = jnp.concatenate(pieces, axis=1)
    full_gate = full[:local_experts]
    full_up = full[local_experts : 2 * local_experts]
    full_down = full[2 * local_experts :]
    gate_pre = jnp.einsum("erd,efd->erf", rows_in, full_gate, preferred_element_type=jnp.float32)
    up_pre = jnp.einsum("erd,efd->erf", rows_in, full_up, preferred_element_type=jnp.float32)
    sigmoid_gate = jax.nn.sigmoid(gate_pre)
    activated = gate_pre * sigmoid_gate
    hidden = (activated * up_pre).astype(jnp.bfloat16)
    out_rows = jnp.einsum(
        "erf,efd->erd", hidden, full_down, preferred_element_type=jnp.float32
    ).astype(jnp.bfloat16)
    d_hidden = jnp.einsum("erd,efd->erf", rows_cot, full_down, preferred_element_type=jnp.float32)
    d_gate = (d_hidden * up_pre * (sigmoid_gate + activated * (1.0 - sigmoid_gate))).astype(
        jnp.bfloat16
    )
    d_up = (d_hidden * activated).astype(jnp.bfloat16)
    dx_rows = jnp.einsum("erf,efd->erd", d_gate, full_gate, preferred_element_type=jnp.float32)
    dx_rows = (
        dx_rows + jnp.einsum("erf,efd->erd", d_up, full_up, preferred_element_type=jnp.float32)
    ).astype(jnp.bfloat16)
    part_down = jnp.einsum("erf,erd->efd", hidden, rows_cot, preferred_element_type=jnp.float32)
    part_gate = jnp.einsum("erf,erd->efd", d_gate, rows_in, preferred_element_type=jnp.float32)
    part_up = jnp.einsum("erf,erd->efd", d_up, rows_in, preferred_element_type=jnp.float32)
    out_rows = out_rows.reshape(local_experts, n_in, 2, slots, width)
    dx_rows = dx_rows.reshape(local_experts, n_in, 2, slots, width)

    def returning(which):
        back = jnp.stack([out_rows[:, :, which], dx_rows[:, :, which]], axis=2)
        back = back.transpose(1, 0, 2, 3, 4).reshape(half_experts, 2, slots, width)
        return lax.all_to_all(back, "inner", split_axis=0, concat_axis=0, tiled=True)

    parts = jnp.concatenate([part_gate, part_up, part_down], axis=0)
    summed = parts[:, :hidden_part]
    for d in range(1, n_dp):
        block = parts[:, d * hidden_part : (d + 1) * hidden_part].astype(jnp.bfloat16)
        summed = summed + shifted(block, "dp", n_dp, -d).astype(jnp.float32)
    summed = summed.astype(jnp.bfloat16)
    grad_gate_w = summed[:local_experts]
    grad_up_w = summed[local_experts : 2 * local_experts]
    grad_down_w = summed[2 * local_experts :]
    place = jnp.where(inside, local * slots + all_code % slots, half_rows)
    columns = jnp.arange(half_rows, dtype=jnp.int32)

    def combine(which):
        back = returning(which)
        out_part = back[:, 0].reshape(half_rows, width)
        dx_part = back[:, 1].reshape(half_rows, width)
        rows = slice(which * tok_rows, (which + 1) * tok_rows)
        hit = place[rows][:, :, None] == columns[None, None, :]
        weight = jnp.sum(jnp.where(hit, all_gates[rows][:, :, None], 0.0), axis=1)
        ones = jnp.sum(hit.astype(jnp.float32), axis=1).astype(jnp.bfloat16)
        layer = jnp.dot(in_three(weight), out_part, preferred_element_type=jnp.float32)
        layer = layer[:tok_rows] + layer[tok_rows : 2 * tok_rows] + layer[2 * tok_rows :]
        grads = jnp.dot(ones, dx_part, preferred_element_type=jnp.float32)
        scores = jnp.dot(all_rows[rows, width:], out_part.T, preferred_element_type=jnp.float32)
        gg = jnp.sum(jnp.where(hit, scores[:, None, :], 0.0), axis=2)
        return (layer, grads, gg)

    partner_layer, partner_grads, partner_gg = combine(1)
    returned = shifted(
        jnp.concatenate([partner_layer, partner_grads], axis=1).astype(jnp.bfloat16), "half", 2, 1
    )
    returned_gg = shifted(partner_gg, "half", 2, 1)
    own_layer, own_grads, own_gg = combine(0)
    layer_out = (own_layer + returned[:, :width].astype(jnp.float32)).astype(jnp.bfloat16)
    grad_tokens = (own_grads + returned[:, width:].astype(jnp.float32)).astype(jnp.bfloat16)
    grad_gates = own_gg + returned_gg
    return (layer_out, grad_tokens, grad_gates, grad_gate_w, grad_up_w, grad_down_w)


def solution(mesh):
    n_expert = mesh.shape["expert"]
    n_dp = mesh.shape["dp"]
    devices = np.asarray(mesh.devices).reshape(2, n_expert // 2, n_dp)
    split = Mesh(devices, ("half", "inner", "dp"))
    rows = P(("half", "inner", "dp"), None)
    weights = P(("half", "inner"), "dp", None)
    return jax.shard_map(
        on_device,
        mesh=split,
        in_specs=(rows, rows, rows, rows, P(), weights, weights, weights),
        out_specs=(rows, rows, rows, weights, weights, weights),
        check_vma=False,
    )
```

profile of v0, /device:TPU:0, one launch (start us, length us, event | category | flops | bytes accessed | tf_op | source)
XLA Modules:
  0.0 487.5 jit_solution(17768026236895901356)
XLA Ops:
  0.7 1.1 constant_dynamic-update-slice_fusion.1
  1.7 1.1 constant_dynamic-update-slice_fusion
  2.8 4.1 collective-permute-start.1
  6.9 0.8 copy.82
  7.9 1.7 reduce-window.6
  10.4 2.9 collective-permute-start.2
  13.7 39.1 %collective-permute-done = s32[128,6]{0,1:T(8,128)S(1)} collective-permute-done((s32[128,6]{0,1:T(8,128)S(1)}, s32[128,6]{0,1:T(8,128)S(1)}, u32[]{:S(2)}, u32[]{:S(2)}) %collective-permute-start) | collective-permute-done | bytes 3104 | tf_op jit(solution)/shard_map/ppermute | solution.py:10
  54.2 6.2 %scatter_custom_fusion = s32[960]{0:T(1024)S(1)} fusion(s32[1536]{0:T(1024)S(1)} %fusion.47, s32[1536]{0:T(1024)S(1)} %reshape.415, s32[]{:T(128)} %constant.25.clone.1), kind=kCustom, calls=%fused_computation.128 | custom fusion | bytes 3844 | tf_op jit(solution)/shard_map/scatter | solution.py:62
  60.4 6.2 %scatter_custom_fusion.1 = f32[960]{0:T(1024)S(1)} fusion(s32[1536]{0:T(1024)S(1)} %fusion.47, f32[1536]{0:T(1024)S(1)} %reshape.423, f32[]{:T(128)} %constant.34.clone.1), kind=kCustom, calls=%fused_computation.126 | custom fusion | bytes 3844 | tf_op jit(solution)/shard_map/scatter | solution.py:67
  66.6 2.2 fusion.7
  68.8 2.6 slice.256
  71.4 2.5 fusion
  73.9 7.4 %pad_maximum_fusion.1 = bf16[960,4096]{1,0:T(8,128)(2,1)} fusion(bf16[960,2048]{1,0:T(8,128)(2,1)} %fusion, bf16[960,2048]{1,0:T(8,128)(2,1)} %slice.256), kind=kLoop, calls=%fused_computation.7 | loop fusion | flops 15728640 | bytes 15728640 | tf_op jit(solution)/shard_map/concatenate | solution.py:75
  81.3 5.1 %all-to-all-start = ((bf16[8,120,4096]{2,1,0:T(8,128)(2,1)}), bf16[8,120,4096]{2,1,0:T(8,128)(2,1)}, u32[]{:S(2)}, u32[]{:S(2)}) async-start(bf16[8,120,4096]{2,1,0:T(8,128)(2,1)} %bitcast.83), calls=%async_computation | async-start | bytes 15728640 | tf_op jit(solution)/shard_map/all_to_all | solution.py:76
  86.5 1.2 constant_dynamic-update-slice_fusion.3
  87.9 1.6 collective-permute-start.3
  89.8 109.6 %psum.7 = f32[16,16]{1,0:T(8,128)S(1)} all-reduce(f32[16,16]{1,0:T(8,128)S(1)} %select_convert_fusion), channel_id=1, replica_groups=mesh['half'=2,'inner'=8,'dp'=2] {'half','inner'}, use_global_device_ids=true, to_apply=%region_4.5 | all-reduce | flops 256 | bytes 2048 | tf_op jit(solution)/shard_map/psum | solution.py:48
  199.7 0.6 gather_fusion
  200.5 0.6 dynamic-slice.6
  201.1 0.7 add_compare_fusion
  201.9 6.9 %bitcast_select_fusion = bf16[1,960,4096]{2,1,0:T(8,128)(2,1)} fusion(pred[960]{0:T(1024)(128)(4,1)S(1)} %lt.80, bf16[1,960,4096]{2,1,0:T(8,128)(2,1)} %bitcast.81), kind=kLoop, calls=%fused_computation.8 | loop fusion | flops 3932160 | bytes 15729600 | tf_op jit(solution)/shard_map/jit(_where)/select_n | solution.py:86
  208.8 4.7 fusion.3
  213.5 3.3 fusion.6
  216.9 4.7 multiply_convert_fusion.2
  221.5 3.6 fusion.61
  225.1 5.3 %add_convert_fusion = bf16[960,2048]{1,0:T(8,128)(2,1)} fusion(f32[960,2048]{1,0:T(8,128)S(1)} %fusion.61, bf16[960,384]{1,0:T(8,128)(2,1)S(1)} %get-tuple-element.45, bf16[3,192,2048]{2,1,0:T(8,128)(2,1)S(1)} %constant_dynamic-update-slice_fusion.2, bf16[3,192,2048]{2,1,0:T(8,128)(2,1)} %collective-permute-done.3), kind=kOutput, calls=%fused_computation.9 | convolution fusion | flops 1517027328 | bytes 17252352 | tf_op jit(solution)/shard_map/erf,efd->erd/dot_general | solution.py:107
  230.4 5.1 %reshape.356 = bf16[1,8,2,60,2048]{4,3,2,1,0:T(8,128)(2,1)} reshape(bf16[960,2048]{1,0:T(8,128)(2,1)} %add_convert_fusion) | data formatting | bytes 7864320 | tf_op jit(solution)/shard_map/reshape | solution.py:115
  235.5 5.4 %convolution_convert_fusion = bf16[960,2048]{1,0:T(8,128)(2,1)} fusion(bf16[960,384]{1,0:T(8,128)(2,1)} %get-tuple-element.44, bf16[3,192,2048]{2,1,0:T(8,128)(2,1)} %collective-permute-done.3, bf16[3,192,2048]{2,1,0:T(8,128)(2,1)S(1)} %constant_dynamic-update-slice_fusion.2), kind=kOutput, calls=%fused_computation.25 | convolution fusion | flops 1515061248 | bytes 9388032 | tf_op jit(solution)/shard_map/erf,efd->erd/dot_general | solution.py:99
  240.9 4.9 %reshape.354 = bf16[1,8,2,60,2048]{4,3,2,1,0:T(8,128)(2,1)} reshape(bf16[960,2048]{1,0:T(8,128)(2,1)} %convolution_convert_fusion) | data formatting | bytes 7864320 | tf_op jit(solution)/shard_map/reshape | solution.py:114
  245.8 4.8 fusion.64
  250.6 0.4 maximum_bitcast_fusion.1
  251.0 6.0 %copy.93 = bf16[8,2,60,2048]{3,1,2,0:T(2,128)(2,1)} copy(bf16[8,2,60,2048]{3,2,1,0:T(8,128)(2,1)S(1)} %maximum_bitcast_fusion.1) | data formatting | bytes 7864320 | tf_op jit(solution)/shard_map/reshape;transpose | solution.py:119
  257.1 4.5 all-to-all-start.2
  261.6 2.0 maximum_bitcast_fusion
  263.6 6.0 %copy.92 = bf16[8,2,60,2048]{3,1,2,0:T(2,128)(2,1)} copy(bf16[8,2,60,2048]{3,2,1,0:T(8,128)(2,1)S(1)} %maximum_bitcast_fusion) | data formatting | bytes 7864320 | tf_op jit(solution)/shard_map/reshape;transpose | solution.py:119
  269.6 37.3 %all-to-all-done.2 = bf16[8,2,60,2048]{3,1,2,0:T(2,128)(2,1)} async-done(((bf16[8,2,60,2048]{3,1,2,0:T(2,128)(2,1)}), bf16[8,2,60,2048]{3,1,2,0:T(2,128)(2,1)}, u32[]{:S(2)}, u32[]{:S(2)}) %all-to-all-start.2) | async-done | bytes 3932192 | tf_op jit(solution)/shard_map/all_to_all | solution.py:120
  306.9 4.9 %all-to-all-start.1 = ((bf16[8,2,60,2048]{3,1,2,0:T(2,128)(2,1)}), bf16[8,2,60,2048]{3,1,2,0:T(2,128)(2,1)}, u32[]{:S(2)}, u32[]{:S(2)}) async-start(bf16[8,2,60,2048]{3,1,2,0:T(2,128)(2,1)} %copy.92), calls=%async_computation.1 | async-start | bytes 7864320 | tf_op jit(solution)/shard_map/all_to_all | solution.py:120
  311.9 4.1 convolution_bitcast_fusion
  316.0 4.1 convolution_bitcast_fusion.1
  320.2 1.8 fusion.4
  322.0 1.2 pad_maximum_fusion
  323.6 1.6 collective-permute-start.6
  325.2 52.1 %collective-permute-done.6 = bf16[3,192,2048]{2,1,0:T(8,128)(2,1)S(1)} collective-permute-done((bf16[3,192,2048]{2,1,0:T(8,128)(2,1)S(1)}, bf16[3,192,2048]{2,1,0:T(8,128)(2,1)S(1)}, u32[]{:S(2)}, u32[]{:S(2)}) %collective-permute-start.6) | collective-permute-done | bytes 2359328 | tf_op jit(solution)/shard_map/ppermute | solution.py:10
  377.2 0.9 fusion.1
  378.1 1.4 fusion.66
  379.6 20.6 %slice_reduce_fusion.2 = (bf16[8,60,2048]{2,1,0:T(8,128)(2,1)}, bf16[8,60,2048]{2,1,0:T(8,128)(2,1)}) fusion(bf16[8,2,60,2048]{3,1,2,0:T(2,128)(2,1)} %all-to-all-done.2), kind=kLoop, calls=%fused_computation.21 | loop fusion | bytes 7864320 | tf_op jit(solution)/shard_map/slice | solution.py:136
  400.2 1.8 reshape_squeeze.13
  402.0 0.7 fusion.20
  402.7 0.4 select_reduce_fusion
  403.3 20.7 %slice_reduce_fusion = (bf16[8,60,2048]{2,1,0:T(8,128)(2,1)}, bf16[8,60,2048]{2,1,0:T(8,128)(2,1)}) fusion(bf16[8,2,60,2048]{3,1,2,0:T(2,128)(2,1)} %all-to-all-done.1), kind=kLoop, calls=%fused_computation.19 | loop fusion | bytes 7864320 | tf_op jit(solution)/shard_map/slice | solution.py:137
  424.0 1.7 reshape_squeeze.12
  425.8 2.5 fusion.29
  428.5 2.7 reshape_squeeze.14
  431.2 2.1 convolution_convert_fusion.1
  433.3 1.1 pad_maximum_fusion.3
  434.4 2.9 collective-permute-start.4
  437.3 0.7 convolution_bitcast_fusion.2
  438.1 0.4 select_reduce_fusion.1
  438.6 2.7 fusion.23
  441.2 2.9 reshape_squeeze.15
  444.1 0.6 add.207
  444.7 38.1 %collective-permute-done.4 = bf16[128,4096]{1,0:T(8,128)(2,1)} collective-permute-done((bf16[128,4096]{1,0:T(8,128)(2,1)}, bf16[128,4096]{1,0:T(8,128)(2,1)}, u32[]{:S(2)}, u32[]{:S(2)}) %collective-permute-start.4) | collective-permute-done | bytes 1048608 | tf_op jit(solution)/shard_map/ppermute | solution.py:10
  482.9 2.1 fusion.19
  485.0 2.3 add_convert_fusion.1
  (91 shorter events, 4.4 us)
Async XLA Ops:
  0.6 9.7 %copy-start.12 = (s32[128,6]{0,1:T(8,128)S(1)}, s32[128,6]{0,1:T(8,128)}, u32[]{:S(2)}) copy-start(s32[128,6]{0,1:T(8,128)} %param.10) | copy-start | bytes 9220
  0.6 9.8 %copy-start.11 = (f32[128,6]{0,1:T(8,128)S(1)}, f32[128,6]{0,1:T(8,128)}, u32[]{:S(2)}) copy-start(f32[128,6]{0,1:T(8,128)} %param.11) | copy-start | bytes 9220
  2.8 63.7 %collective-permute-start.1 = (bf16[128,4096]{1,0:T(8,128)(2,1)S(1)}, bf16[128,4096]{1,0:T(8,128)(2,1)S(1)}, u32[]{:S(2)}, u32[]{:S(2)}) collective-permute-start(bf16[128,4096]{1,0:T(8,128)(2,1)S(1)} %constant_dynamic-update-slice_fusion), channel_id=1, source_target_pairs={{0,16},{16,0},{1,17},{17,1},{2,18},{18,2},{3,19},{19,3},{4,20},{20... | collective-permute-start | bytes 3145736 | tf_op jit(solution)/shard_map/ppermute | solution.py:10
  10.3 42.5 %collective-permute-start = (s32[128,6]{0,1:T(8,128)S(1)}, s32[128,6]{0,1:T(8,128)S(1)}, u32[]{:S(2)}, u32[]{:S(2)}) collective-permute-start(s32[128,6]{0,1:T(8,128)S(1)} %multiply_add_fusion), channel_id=1, source_target_pairs={{0,16},{16,0},{1,17},{17,1},{2,18},{18,2},{3,19},{19,3},{4,20},{20... | collective-permute-start | bytes 9224 | tf_op jit(solution)/shard_map/ppermute | solution.py:10
  10.4 43.4 %collective-permute-start.2 = (f32[128,6]{0,1:T(8,128)S(1)}, f32[128,6]{0,1:T(8,128)S(1)}, u32[]{:S(2)}, u32[]{:S(2)}) collective-permute-start(f32[128,6]{0,1:T(8,128)S(1)} %copy-done.11), channel_id=1, source_target_pairs={{0,16},{16,0},{1,17},{17,1},{2,18},{18,2},{3,19},{19,3},{4,20},{20... | collective-permute-start | bytes 9224 | tf_op jit(solution)/shard_map/ppermute | solution.py:10
  66.6 2.3 copy-start.4
  81.3 5.1 %copy-start.7 = (bf16[1,192,2048]{2,1,0:T(8,128)(2,1)S(1)}, bf16[1,192,2048]{2,1,0:T(8,128)(2,1)}, u32[]{:S(2)}) copy-start(bf16[1,192,2048]{2,1,0:T(8,128)(2,1)} %param.13) | copy-start | bytes 2359300
  81.3 120.6 %all-to-all-start = ((bf16[8,120,4096]{2,1,0:T(8,128)(2,1)}), bf16[8,120,4096]{2,1,0:T(8,128)(2,1)}, u32[]{:S(2)}, u32[]{:S(2)}) async-start(bf16[8,120,4096]{2,1,0:T(8,128)(2,1)} %bitcast.83), calls=%async_computation | async-start | bytes 15728640 | tf_op jit(solution)/shard_map/all_to_all | solution.py:76
  86.4 1.4 copy-start.8
  86.4 114.0 %copy-start.13 = (s32[16]{0:T(128)S(1)}, s32[16]{0:T(128)}, u32[]{:S(2)}) copy-start(s32[16]{0:T(128)} %param.12) | copy-start | bytes 196
  87.9 121.0 %collective-permute-start.3 = (bf16[3,192,2048]{2,1,0:T(8,128)(2,1)S(1)}, bf16[3,192,2048]{2,1,0:T(8,128)(2,1)}, u32[]{:S(2)}, u32[]{:S(2)}) collective-permute-start(bf16[3,192,2048]{2,1,0:T(8,128)(2,1)S(1)} %constant_dynamic-update-slice_fusion.2), channel_id=1, source_target_pairs={{0,1},{1,0},{2,3},{3,2},{4,5},{5,4},{6,7},{7,6},{8,9},{9,8},{10,11... | collective-permute-start | bytes 7077896 | tf_op jit(solution)/shard_map/ppermute | solution.py:10
  208.8 4.7 copy-start.2
  221.5 3.6 copy-start.9
  257.1 49.9 %all-to-all-start.2 = ((bf16[8,2,60,2048]{3,1,2,0:T(2,128)(2,1)}), bf16[8,2,60,2048]{3,1,2,0:T(2,128)(2,1)}, u32[]{:S(2)}, u32[]{:S(2)}) async-start(bf16[8,2,60,2048]{3,1,2,0:T(2,128)(2,1)} %copy.93), calls=%async_computation.2 | async-start | bytes 7864320 | tf_op jit(solution)/shard_map/all_to_all | solution.py:120
  306.9 96.3 %all-to-all-start.1 = ((bf16[8,2,60,2048]{3,1,2,0:T(2,128)(2,1)}), bf16[8,2,60,2048]{3,1,2,0:T(2,128)(2,1)}, u32[]{:S(2)}, u32[]{:S(2)}) async-start(bf16[8,2,60,2048]{3,1,2,0:T(2,128)(2,1)} %copy.92), calls=%async_computation.1 | async-start | bytes 7864320 | tf_op jit(solution)/shard_map/all_to_all | solution.py:120
  311.9 4.1 copy-start.10
  311.9 8.3 %slice-start = ((s8[7864320]{0:T(1024)(128)(4,1)}), s8[4194304]{0:T(1024)(128)(4,1)S(1)}, s32[]{:S(2)}) async-start(s8[7864320]{0:T(1024)(128)(4,1)} %bitcast.84), calls=%async_computation.3 | async-start | bytes 8388608
  316.0 4.2 slice-start.1
  316.0 4.2 copy-start.14
  323.6 53.7 %collective-permute-start.6 = (bf16[3,192,2048]{2,1,0:T(8,128)(2,1)S(1)}, bf16[3,192,2048]{2,1,0:T(8,128)(2,1)S(1)}, u32[]{:S(2)}, u32[]{:S(2)}) collective-permute-start(bf16[3,192,2048]{2,1,0:T(8,128)(2,1)S(1)} %slice.257), channel_id=1, source_target_pairs={{0,1},{1,0},{2,3},{3,2},{4,5},{5,4},{6,7},{7,6},{8,9},{9,8},{10,11... | collective-permute-start | bytes 7077896 | tf_op jit(solution)/shard_map/ppermute | solution.py:10
  400.2 1.9 copy-start.5
  402.0 21.9 %copy-start = (bf16[480,2048]{1,0:T(8,128)(2,1)}, bf16[480,2048]{1,0:T(8,128)(2,1)S(1)}, u32[]{:S(2)}) copy-start(bf16[480,2048]{1,0:T(8,128)(2,1)S(1)} %reshape_squeeze.13) | copy-start | bytes 5898244
  403.2 41.0 %collective-permute-start.5 = (f32[128,6]{0,1:T(8,128)S(1)}, f32[128,6]{0,1:T(8,128)S(1)}, u32[]{:S(2)}, u32[]{:S(2)}) collective-permute-start(f32[128,6]{0,1:T(8,128)S(1)} %get-tuple-element.32), channel_id=1, source_target_pairs={{0,16},{16,0},{1,17},{17,1},{2,18},{18,2},{3,19},{19,3},{4,20},{20... | collective-permute-start | bytes 9224 | tf_op jit(solution)/shard_map/ppermute | solution.py:10
  431.2 6.1 %copy-start.6 = (bf16[128,2048]{1,0:T(8,128)(2,1)S(1)}, bf16[128,2048]{1,0:T(8,128)(2,1)}, u32[]{:S(2)}) copy-start(bf16[128,2048]{1,0:T(8,128)(2,1)} %param.9) | copy-start | bytes 1572868
  434.4 48.4 %collective-permute-start.4 = (bf16[128,4096]{1,0:T(8,128)(2,1)}, bf16[128,4096]{1,0:T(8,128)(2,1)}, u32[]{:S(2)}, u32[]{:S(2)}) collective-permute-start(bf16[128,4096]{1,0:T(8,128)(2,1)} %pad_maximum_fusion.3), channel_id=1, source_target_pairs={{0,16},{16,0},{1,17},{17,1},{2,18},{18,2},{3,19},{19,3},{4,20},{20... | collective-permute-start | bytes 3145736 | tf_op jit(solution)/shard_map/ppermute | solution.py:10
  441.2 41.6 %copy-start.1 = (f32[384,2048]{1,0:T(8,128)S(1)}, f32[384,2048]{1,0:T(8,128)}, u32[]{:S(2)}) copy-start(f32[384,2048]{1,0:T(8,128)} %fusion.23) | copy-start | bytes 9437188
  444.1 40.9 %copy-start.3 = (bf16[480,2048]{1,0:T(8,128)(2,1)S(1)}, bf16[480,2048]{1,0:T(8,128)(2,1)}, u32[]{:S(2)}) copy-start(bf16[480,2048]{1,0:T(8,128)(2,1)} %reshape_squeeze.15) | copy-start | bytes 5898244
where the time goes:
time: 495 us; the launch traced here: 487 us
  waiting for transfers between devices  167 us (34%)
  blocking collectives  110 us (22%)
  local copies, waits for them, and re-layouts  103 us (21%)
  matrix products  50.3 us (10%)
  other arithmetic  29.1 us (6%)
  starting transfers between devices  27.9 us (6%)
    ppermute x7, waiting for transfers between devices, shifted(): lax.ppermute(value, axis, [(j, (j + shift) % count) for j in range(count)])  129 us
    psum x1, blocking collectives, on_device(): lax.psum(count_rows.astype(jnp.float32), ('half', 'inner'))  110 us
    all_to_all x2, waiting for transfers between devices, returning(): lax.all_to_all(back, 'inner', split_axis=0, concat_axis=0, tiled=True)  37.3 us
    slice x1, local copies, waits for them, and re-layouts, combine(): dx_part = back[:, 1].reshape(half_rows, width)  20.7 us
    slice x1, local copies, waits for them, and re-layouts, combine(): out_part = back[:, 0].reshape(half_rows, width)  20.6 us
    ppermute x7, starting transfers between devices, shifted(): lax.ppermute(value, axis, [(j, (j + shift) % count) for j in range(count)])  13.3 us
    another operation x2, local copies, waits for them, and re-layouts, returning(): back = back.transpose(1, 0, 2, 3, 4).reshape(half_experts, 2, slots, width)  12.1 us
  transfers between devices with their start and end apart: 10, of which 4 were waited for; matrix products, arithmetic and copies ran while one was open for 23% of the time, Pallas kernels for 0%

commit v1 on v0

--- a/solution.py
+++ b/solution.py
@@ -45,7 +45,9 @@
     count_rows = jnp.where(
         jnp.arange(n_src, dtype=jnp.int32)[:, None] == source, counts[None, :], 0
     )
-    all_counts = lax.psum(count_rows.astype(jnp.float32), ("half", "inner")).astype(jnp.int32)
+    all_counts = lax.psum(lax.psum(count_rows.astype(jnp.float32), "inner"), "half").astype(
+        jnp.int32
+    )
     code = (flat_ids * slots + local_rank).reshape(tok_rows, top_count)
     partner_code = shifted(code, "half", 2, 1)
     all_rows = jnp.concatenate([both_rows, partner_rows], axis=0)

time: 495 us -> 484 us (0.978)
  blocking collectives: 110 us -> 97.7 us
    psum x1 -> x2, blocking collectives: 110 us -> 97.7 us  [the longest x1 91.6 us: on_device(): lax.psum(count_rows.astype(jnp.float32), 'inner')]
  transfers between devices with their start and end apart: 10 -> 10, of which waited for: 4 -> 4; matrix products, arithmetic and copies ran while one was open for 23% -> 24% of each run, Pallas kernels for 0% -> 0%
where the time goes in v1:
time: 484 us; the launch traced here: 477 us
  waiting for transfers between devices  168 us (35%)
  local copies, waits for them, and re-layouts  103 us (21%)
  blocking collectives  97.7 us (20%)
  matrix products  50.3 us (10%)
  other arithmetic  29.1 us (6%)
  starting transfers between devices  27.9 us (6%)
    ppermute x7, waiting for transfers between devices, shifted(): lax.ppermute(value, axis, [(j, (j + shift) % count) for j in range(count)])  130 us
    psum x1, blocking collectives, on_device(): lax.psum(count_rows.astype(jnp.float32), 'inner')  91.6 us
    all_to_all x2, waiting for transfers between devices, returning(): lax.all_to_all(back, 'inner', split_axis=0, concat_axis=0, tiled=True)  37.3 us
    slice x1, local copies, waits for them, and re-layouts, combine(): dx_part = back[:, 1].reshape(half_rows, width)  20.7 us
    slice x1, local copies, waits for them, and re-layouts, combine(): out_part = back[:, 0].reshape(half_rows, width)  20.6 us
    ppermute x7, starting transfers between devices, shifted(): lax.ppermute(value, axis, [(j, (j + shift) % count) for j in range(count)])  13.3 us
    another operation x2, local copies, waits for them, and re-layouts, returning(): back = back.transpose(1, 0, 2, 3, 4).reshape(half_experts, 2, slots, width)  12.1 us
  transfers between devices with their start and end apart: 10, of which 4 were waited for; matrix products, arithmetic and copies ran while one was open for 24% of the time, Pallas kernels for 0%

profile of v1, /device:TPU:0, one launch (start us, length us, event | category | flops | bytes accessed | tf_op | source)
XLA Modules:
  0.0 476.7 jit_solution(10421052450713779993)
XLA Ops:
  0.7 1.1 constant_dynamic-update-slice_fusion.1
  1.7 1.1 constant_dynamic-update-slice_fusion
  2.8 4.1 collective-permute-start.1
  6.9 0.8 copy.82
  7.9 1.7 reduce-window.6
  10.4 2.9 collective-permute-start.2
  13.7 39.1 %collective-permute-done = s32[128,6]{0,1:T(8,128)S(1)} collective-permute-done((s32[128,6]{0,1:T(8,128)S(1)}, s32[128,6]{0,1:T(8,128)S(1)}, u32[]{:S(2)}, u32[]{:S(2)}) %collective-permute-start) | collective-permute-done | bytes 3104 | tf_op jit(solution)/shard_map/ppermute | solution.py:10
  54.2 6.2 %scatter_custom_fusion = s32[960]{0:T(1024)S(1)} fusion(s32[1536]{0:T(1024)S(1)} %fusion.47, s32[1536]{0:T(1024)S(1)} %reshape.415, s32[]{:T(128)} %constant.25.clone.1), kind=kCustom, calls=%fused_computation.128 | custom fusion | bytes 3844 | tf_op jit(solution)/shard_map/scatter | solution.py:64
  60.4 6.2 %scatter_custom_fusion.1 = f32[960]{0:T(1024)S(1)} fusion(s32[1536]{0:T(1024)S(1)} %fusion.47, f32[1536]{0:T(1024)S(1)} %reshape.423, f32[]{:T(128)} %constant.34.clone.1), kind=kCustom, calls=%fused_computation.126 | custom fusion | bytes 3844 | tf_op jit(solution)/shard_map/scatter | solution.py:69
  66.6 2.2 fusion.7
  68.8 2.6 slice.256
  71.4 2.5 fusion
  73.9 7.4 %pad_maximum_fusion.1 = bf16[960,4096]{1,0:T(8,128)(2,1)} fusion(bf16[960,2048]{1,0:T(8,128)(2,1)} %fusion, bf16[960,2048]{1,0:T(8,128)(2,1)} %slice.256), kind=kLoop, calls=%fused_computation.7 | loop fusion | flops 15728640 | bytes 15728640 | tf_op jit(solution)/shard_map/concatenate | solution.py:77
  81.3 5.1 %all-to-all-start = ((bf16[8,120,4096]{2,1,0:T(8,128)(2,1)}), bf16[8,120,4096]{2,1,0:T(8,128)(2,1)}, u32[]{:S(2)}, u32[]{:S(2)}) async-start(bf16[8,120,4096]{2,1,0:T(8,128)(2,1)} %bitcast.83), calls=%async_computation | async-start | bytes 15728640 | tf_op jit(solution)/shard_map/all_to_all | solution.py:78
  86.5 1.2 constant_dynamic-update-slice_fusion.3
  87.9 1.6 collective-permute-start.3
  89.8 91.6 %psum.14 = f32[16,16]{1,0:T(8,128)S(1)} all-reduce(f32[16,16]{1,0:T(8,128)S(1)} %select_convert_fusion), channel_id=1, replica_groups=mesh['half'=2,'inner'=8,'dp'=2] {'inner'}, use_global_device_ids=true, to_apply=%region_4.5 | all-reduce | flops 256 | bytes 2048 | tf_op jit(solution)/shard_map/psum | solution.py:48
  181.5 6.1 %psum.15 = f32[16,16]{1,0:T(8,128)S(1)} all-reduce(f32[16,16]{1,0:T(8,128)S(1)} %psum.14), channel_id=1, replica_groups=mesh['half'=2,'inner'=8,'dp'=2] {'half'}, use_global_device_ids=true, to_apply=%region_5.6 | all-reduce | flops 256 | bytes 2048 | tf_op jit(solution)/shard_map/psum | solution.py:48
  187.8 0.6 gather_fusion
  188.6 0.6 dynamic-slice.6
  189.2 0.7 add_compare_fusion
  190.0 6.9 %bitcast_select_fusion = bf16[1,960,4096]{2,1,0:T(8,128)(2,1)} fusion(pred[960]{0:T(1024)(128)(4,1)S(1)} %lt.80, bf16[1,960,4096]{2,1,0:T(8,128)(2,1)} %bitcast.81), kind=kLoop, calls=%fused_computation.8 | loop fusion | flops 3932160 | bytes 15729600 | tf_op jit(solution)/shard_map/jit(_where)/select_n | solution.py:88
  196.9 4.7 fusion.3
  201.6 3.3 fusion.6
  205.0 4.7 multiply_convert_fusion.2
  209.6 3.6 fusion.61
  213.2 5.3 %add_convert_fusion = bf16[960,2048]{1,0:T(8,128)(2,1)} fusion(f32[960,2048]{1,0:T(8,128)S(1)} %fusion.61, bf16[960,384]{1,0:T(8,128)(2,1)S(1)} %get-tuple-element.45, bf16[3,192,2048]{2,1,0:T(8,128)(2,1)S(1)} %constant_dynamic-update-slice_fusion.2, bf16[3,192,2048]{2,1,0:T(8,128)(2,1)} %collective-permute-done.3), kind=kOutput, calls=%fused_computation.9 | convolution fusion | flops 1517027328 | bytes 17252352 | tf_op jit(solution)/shard_map/erf,efd->erd/dot_general | solution.py:109
  218.5 5.1 %reshape.356 = bf16[1,8,2,60,2048]{4,3,2,1,0:T(8,128)(2,1)} reshape(bf16[960,2048]{1,0:T(8,128)(2,1)} %add_convert_fusion) | data formatting | bytes 7864320 | tf_op jit(solution)/shard_map/reshape | solution.py:117
  223.6 5.4 %convolution_convert_fusion = bf16[960,2048]{1,0:T(8,128)(2,1)} fusion(bf16[960,384]{1,0:T(8,128)(2,1)} %get-tuple-element.44, bf16[3,192,2048]{2,1,0:T(8,128)(2,1)} %collective-permute-done.3, bf16[3,192,2048]{2,1,0:T(8,128)(2,1)S(1)} %constant_dynamic-update-slice_fusion.2), kind=kOutput, calls=%fused_computation.25 | convolution fusion | flops 1515061248 | bytes 9388032 | tf_op jit(solution)/shard_map/erf,efd->erd/dot_general | solution.py:101
  229.0 4.9 %reshape.354 = bf16[1,8,2,60,2048]{4,3,2,1,0:T(8,128)(2,1)} reshape(bf16[960,2048]{1,0:T(8,128)(2,1)} %convolution_convert_fusion) | data formatting | bytes 7864320 | tf_op jit(solution)/shard_map/reshape | solution.py:116
  234.0 4.8 %fusion.64 = (bf16[1,8,1,60,2048]{4,3,2,1,0:T(8,128)(2,1)S(1)}, bf16[1,8,1,60,2048]{4,3,2,1,0:T(8,128)(2,1)S(1)}, bf16[1,8,1,60,2048]{4,3,2,1,0:T(8,128)(2,1)}, bf16[1,8,1,60,2048]{4,3,2,1,0:T(8,128)(2,1)S(1)}) fusion(bf16[1,8,2,60,2048]{4,3,2,1,0:T(8,128)(2,1)} %reshape.354, bf16[1,8,2,60,2048]{4,3,2,1,0:T(8,128)(2,1)} %reshape.356), kind=kLoop, calls=%fused_computation.140 | loop fusion | bytes 15728640 | tf_op jit(solution)/shard_map/slice | solution.py:120
  239.1 6.0 %copy.93 = bf16[8,2,60,2048]{3,1,2,0:T(2,128)(2,1)} copy(bf16[8,2,60,2048]{3,2,1,0:T(8,128)(2,1)S(1)} %maximum_bitcast_fusion.1) | data formatting | bytes 7864320 | tf_op jit(solution)/shard_map/reshape;transpose | solution.py:121
  245.2 4.5 all-to-all-start.2
  249.7 2.0 maximum_bitcast_fusion
  251.7 6.0 %copy.92 = bf16[8,2,60,2048]{3,1,2,0:T(2,128)(2,1)} copy(bf16[8,2,60,2048]{3,2,1,0:T(8,128)(2,1)S(1)} %maximum_bitcast_fusion) | data formatting | bytes 7864320 | tf_op jit(solution)/shard_map/reshape;transpose | solution.py:121
  257.7 37.3 %all-to-all-done.2 = bf16[8,2,60,2048]{3,1,2,0:T(2,128)(2,1)} async-done(((bf16[8,2,60,2048]{3,1,2,0:T(2,128)(2,1)}), bf16[8,2,60,2048]{3,1,2,0:T(2,128)(2,1)}, u32[]{:S(2)}, u32[]{:S(2)}) %all-to-all-start.2) | async-done | bytes 3932192 | tf_op jit(solution)/shard_map/all_to_all | solution.py:122
  295.0 4.9 %all-to-all-start.1 = ((bf16[8,2,60,2048]{3,1,2,0:T(2,128)(2,1)}), bf16[8,2,60,2048]{3,1,2,0:T(2,128)(2,1)}, u32[]{:S(2)}, u32[]{:S(2)}) async-start(bf16[8,2,60,2048]{3,1,2,0:T(2,128)(2,1)} %copy.92), calls=%async_computation.1 | async-start | bytes 7864320 | tf_op jit(solution)/shard_map/all_to_all | solution.py:122
  300.0 4.1 convolution_bitcast_fusion
  304.2 4.1 convolution_bitcast_fusion.1
  308.3 1.8 fusion.4
  310.1 1.2 pad_maximum_fusion
  311.7 1.6 collective-permute-start.6
  313.3 52.0 %collective-permute-done.6 = bf16[3,192,2048]{2,1,0:T(8,128)(2,1)S(1)} collective-permute-done((bf16[3,192,2048]{2,1,0:T(8,128)(2,1)S(1)}, bf16[3,192,2048]{2,1,0:T(8,128)(2,1)S(1)}, u32[]{:S(2)}, u32[]{:S(2)}) %collective-permute-start.6) | collective-permute-done | bytes 2359328 | tf_op jit(solution)/shard_map/ppermute | solution.py:10
  365.3 0.9 fusion.1
  366.2 1.4 fusion.66
  367.7 20.6 %slice_reduce_fusion.2 = (bf16[8,60,2048]{2,1,0:T(8,128)(2,1)}, bf16[8,60,2048]{2,1,0:T(8,128)(2,1)}) fusion(bf16[8,2,60,2048]{3,1,2,0:T(2,128)(2,1)} %all-to-all-done.2), kind=kLoop, calls=%fused_computation.21 | loop fusion | bytes 7864320 | tf_op jit(solution)/shard_map/slice | solution.py:138
  388.3 1.8 reshape_squeeze.13
  390.1 0.7 fusion.20
  391.3 1.5 collective-permute-start.5
  392.8 20.7 %slice_reduce_fusion = (bf16[8,60,2048]{2,1,0:T(8,128)(2,1)}, bf16[8,60,2048]{2,1,0:T(8,128)(2,1)}) fusion(bf16[8,2,60,2048]{3,1,2,0:T(2,128)(2,1)} %all-to-all-done.1), kind=kLoop, calls=%fused_computation.19 | loop fusion | bytes 7864320 | tf_op jit(solution)/shard_map/slice | solution.py:139
  413.5 1.7 reshape_squeeze.12
  415.3 2.5 fusion.29
  418.0 2.7 reshape_squeeze.14
  420.8 2.1 convolution_convert_fusion.1
  422.9 1.1 pad_maximum_fusion.3
  424.0 1.5 collective-permute-start.4
  425.4 0.7 convolution_bitcast_fusion.2
  426.2 0.4 select_reduce_fusion.1
  426.7 2.7 fusion.23
  429.3 2.9 reshape_squeeze.15
  432.2 0.6 add.209
  432.8 39.3 %collective-permute-done.4 = bf16[128,4096]{1,0:T(8,128)(2,1)} collective-permute-done((bf16[128,4096]{1,0:T(8,128)(2,1)}, bf16[128,4096]{1,0:T(8,128)(2,1)}, u32[]{:S(2)}, u32[]{:S(2)}) %collective-permute-start.4) | collective-permute-done | bytes 1048608 | tf_op jit(solution)/shard_map/ppermute | solution.py:10
  472.1 2.1 fusion.19
  474.2 2.3 add_convert_fusion.1
  (92 shorter events, 5.2 us)
Async XLA Ops:
  0.6 9.7 %copy-start.12 = (s32[128,6]{0,1:T(8,128)S(1)}, s32[128,6]{0,1:T(8,128)}, u32[]{:S(2)}) copy-start(s32[128,6]{0,1:T(8,128)} %param.10) | copy-start | bytes 9220
  0.6 9.8 %copy-start.11 = (f32[128,6]{0,1:T(8,128)S(1)}, f32[128,6]{0,1:T(8,128)}, u32[]{:S(2)}) copy-start(f32[128,6]{0,1:T(8,128)} %param.11) | copy-start | bytes 9220
  2.8 63.7 %collective-permute-start.1 = (bf16[128,4096]{1,0:T(8,128)(2,1)S(1)}, bf16[128,4096]{1,0:T(8,128)(2,1)S(1)}, u32[]{:S(2)}, u32[]{:S(2)}) collective-permute-start(bf16[128,4096]{1,0:T(8,128)(2,1)S(1)} %constant_dynamic-update-slice_fusion), channel_id=1, source_target_pairs={{0,16},{16,0},{1,17},{17,1},{2,18},{18,2},{3,19},{19,3},{4,20},{20... | collective-permute-start | bytes 3145736 | tf_op jit(solution)/shard_map/ppermute | solution.py:10
  10.3 42.5 %collective-permute-start = (s32[128,6]{0,1:T(8,128)S(1)}, s32[128,6]{0,1:T(8,128)S(1)}, u32[]{:S(2)}, u32[]{:S(2)}) collective-permute-start(s32[128,6]{0,1:T(8,128)S(1)} %multiply_add_fusion), channel_id=1, source_target_pairs={{0,16},{16,0},{1,17},{17,1},{2,18},{18,2},{3,19},{19,3},{4,20},{20... | collective-permute-start | bytes 9224 | tf_op jit(solution)/shard_map/ppermute | solution.py:10
  10.4 43.4 %collective-permute-start.2 = (f32[128,6]{0,1:T(8,128)S(1)}, f32[128,6]{0,1:T(8,128)S(1)}, u32[]{:S(2)}, u32[]{:S(2)}) collective-permute-start(f32[128,6]{0,1:T(8,128)S(1)} %copy-done.11), channel_id=1, source_target_pairs={{0,16},{16,0},{1,17},{17,1},{2,18},{18,2},{3,19},{19,3},{4,20},{20... | collective-permute-start | bytes 9224 | tf_op jit(solution)/shard_map/ppermute | solution.py:10
  66.6 2.3 copy-start.4
  81.3 5.1 %copy-start.7 = (bf16[1,192,2048]{2,1,0:T(8,128)(2,1)S(1)}, bf16[1,192,2048]{2,1,0:T(8,128)(2,1)}, u32[]{:S(2)}) copy-start(bf16[1,192,2048]{2,1,0:T(8,128)(2,1)} %param.13) | copy-start | bytes 2359300
  81.3 108.7 %all-to-all-start = ((bf16[8,120,4096]{2,1,0:T(8,128)(2,1)}), bf16[8,120,4096]{2,1,0:T(8,128)(2,1)}, u32[]{:S(2)}, u32[]{:S(2)}) async-start(bf16[8,120,4096]{2,1,0:T(8,128)(2,1)} %bitcast.83), calls=%async_computation | async-start | bytes 15728640 | tf_op jit(solution)/shard_map/all_to_all | solution.py:78
  86.4 1.4 copy-start.8
  86.4 102.1 %copy-start.13 = (s32[16]{0:T(128)S(1)}, s32[16]{0:T(128)}, u32[]{:S(2)}) copy-start(s32[16]{0:T(128)} %param.12) | copy-start | bytes 196
  87.9 109.1 %collective-permute-start.3 = (bf16[3,192,2048]{2,1,0:T(8,128)(2,1)S(1)}, bf16[3,192,2048]{2,1,0:T(8,128)(2,1)}, u32[]{:S(2)}, u32[]{:S(2)}) collective-permute-start(bf16[3,192,2048]{2,1,0:T(8,128)(2,1)S(1)} %constant_dynamic-update-slice_fusion.2), channel_id=1, source_target_pairs={{0,1},{1,0},{2,3},{3,2},{4,5},{5,4},{6,7},{7,6},{8,9},{9,8},{10,11... | collective-permute-start | bytes 7077896 | tf_op jit(solution)/shard_map/ppermute | solution.py:10
  196.9 4.7 copy-start.2
  209.6 3.6 copy-start.9
  245.2 49.9 %all-to-all-start.2 = ((bf16[8,2,60,2048]{3,1,2,0:T(2,128)(2,1)}), bf16[8,2,60,2048]{3,1,2,0:T(2,128)(2,1)}, u32[]{:S(2)}, u32[]{:S(2)}) async-start(bf16[8,2,60,2048]{3,1,2,0:T(2,128)(2,1)} %copy.93), calls=%async_computation.2 | async-start | bytes 7864320 | tf_op jit(solution)/shard_map/all_to_all | solution.py:122
  295.0 97.8 %all-to-all-start.1 = ((bf16[8,2,60,2048]{3,1,2,0:T(2,128)(2,1)}), bf16[8,2,60,2048]{3,1,2,0:T(2,128)(2,1)}, u32[]{:S(2)}, u32[]{:S(2)}) async-start(bf16[8,2,60,2048]{3,1,2,0:T(2,128)(2,1)} %copy.92), calls=%async_computation.1 | async-start | bytes 7864320 | tf_op jit(solution)/shard_map/all_to_all | solution.py:122
  300.0 4.1 copy-start.10
  300.0 8.3 %slice-start = ((s8[7864320]{0:T(1024)(128)(4,1)}), s8[4194304]{0:T(1024)(128)(4,1)S(1)}, s32[]{:S(2)}) async-start(s8[7864320]{0:T(1024)(128)(4,1)} %bitcast.84), calls=%async_computation.3 | async-start | bytes 8388608
  304.1 4.2 slice-start.1
  304.1 4.2 copy-start.14
  311.7 53.7 %collective-permute-start.6 = (bf16[3,192,2048]{2,1,0:T(8,128)(2,1)S(1)}, bf16[3,192,2048]{2,1,0:T(8,128)(2,1)S(1)}, u32[]{:S(2)}, u32[]{:S(2)}) collective-permute-start(bf16[3,192,2048]{2,1,0:T(8,128)(2,1)S(1)} %slice.257), channel_id=1, source_target_pairs={{0,1},{1,0},{2,3},{3,2},{4,5},{5,4},{6,7},{7,6},{8,9},{9,8},{10,11... | collective-permute-start | bytes 7077896 | tf_op jit(solution)/shard_map/ppermute | solution.py:10
  388.3 1.9 copy-start.5
  390.1 23.4 %copy-start = (bf16[480,2048]{1,0:T(8,128)(2,1)}, bf16[480,2048]{1,0:T(8,128)(2,1)S(1)}, u32[]{:S(2)}) copy-start(bf16[480,2048]{1,0:T(8,128)(2,1)S(1)} %reshape_squeeze.13) | copy-start | bytes 5898244
  391.3 41.0 %collective-permute-start.5 = (f32[128,6]{0,1:T(8,128)S(1)}, f32[128,6]{0,1:T(8,128)S(1)}, u32[]{:S(2)}, u32[]{:S(2)}) collective-permute-start(f32[128,6]{0,1:T(8,128)S(1)} %get-tuple-element.32), channel_id=1, source_target_pairs={{0,16},{16,0},{1,17},{17,1},{2,18},{18,2},{3,19},{19,3},{4,20},{20... | collective-permute-start | bytes 9224 | tf_op jit(solution)/shard_map/ppermute | solution.py:10
  420.8 4.7 copy-start.6
  424.0 48.1 %collective-permute-start.4 = (bf16[128,4096]{1,0:T(8,128)(2,1)}, bf16[128,4096]{1,0:T(8,128)(2,1)}, u32[]{:S(2)}, u32[]{:S(2)}) collective-permute-start(bf16[128,4096]{1,0:T(8,128)(2,1)} %pad_maximum_fusion.3), channel_id=1, source_target_pairs={{0,16},{16,0},{1,17},{17,1},{2,18},{18,2},{3,19},{19,3},{4,20},{20... | collective-permute-start | bytes 3145736 | tf_op jit(solution)/shard_map/ppermute | solution.py:10
  429.3 42.8 %copy-start.1 = (f32[384,2048]{1,0:T(8,128)S(1)}, f32[384,2048]{1,0:T(8,128)}, u32[]{:S(2)}) copy-start(f32[384,2048]{1,0:T(8,128)} %fusion.23) | copy-start | bytes 9437188
  432.2 42.0 %copy-start.3 = (bf16[480,2048]{1,0:T(8,128)(2,1)S(1)}, bf16[480,2048]{1,0:T(8,128)(2,1)}, u32[]{:S(2)}) copy-start(bf16[480,2048]{1,0:T(8,128)(2,1)} %reshape_squeeze.15) | copy-start | bytes 5898244
